TPU v7x, 32 devices: a whole 2x2x4 slice. The times are simulated.
32 devices in a mesh: grp: 2 (over y), row: 8 (over z, x), chan: 2 (over core).
Axes of the slice: x: 2, y: 2, z: 4, core: 2. Of those that a mesh axis runs over, the one named last changes fastest.
Arguments:
- band_strip: bfloat16 [424, 64, 128], P('chan', ('grp', 'row')), parts along dimension 1, may hold values from -6 to 6
- conv_weight: bfloat16 [1024, 9, 424], P('row', None, 'chan'), may hold values from -0.09375 to 0.09375
- gdn_gamma: bfloat16 [1024, 1024], P('chan'), as said below
- gdn_beta: float32 [1024], P('chan'), may hold values from 0.5 to 2
- cotangent: bfloat16 [1024, 64, 128], P('chan', ('grp', 'row')), parts along dimension 1, may hold values from -6 to 6
Outputs:
- latent: bfloat16 [1024, 64, 128], P('chan', ('grp', 'row')), parts along dimension 1
- grad_strip: float32 [424, 64, 128], P('chan', ('grp', 'row')), parts along dimension 1
- grad_gamma: float32 [2048, 1024], P(('grp', 'chan')), parts along dimension 0
- grad_beta: float32 [2048], P(('grp', 'chan')), parts along dimension 0
There are 2 independent parts, one for each index of `grp`. A program takes and returns all parts, laid end to end along the dimension named above; an argument that names none is the same for every part. Nothing has to cross between parts.
Inputs may be any that keep to these rules, and one draw needn't show every extreme that they name: `gdn_gamma`: gamma's entries are non-negative.
All inputs are finite; a program needn't handle non-finite values.
Results may differ from a plain program's by a relative error of at most 0.0054.
Values may be sent and summed in bfloat16 or wider, within the bound.
No kernel may reach another device: no remote copies, remote signals or barrier semaphores. Data moves between devices by JAX's collectives and lax.ppermute only.
A program may use at most 64 MiB of HBM per device.

v0:
```python
import math
import jax
import jax.numpy as jnp
from jax import lax
from jax.sharding import PartitionSpec as P

TAPS = ((-1, -1), (-1, 0), (-1, 1), (0, -1), (0, 0), (0, 1), (1, -1), (1, 0), (1, 1))


def extended(shard, sides, width):
    for axis, dim in sides:
        count, length = (lax.axis_size(axis), shard.shape[dim])
        up = [(i, (i + 1) % count) for i in range(count - 1)]
        down = [(j, i) for i, j in up]
        last = lax.slice_in_dim(shard, length - width, length, axis=dim)
        leading = lax.slice_in_dim(shard, 0, width, axis=dim)
        before = lax.ppermute(last, axis, up)
        after = lax.ppermute(leading, axis, down)
        shard = jnp.concatenate([before, shard, after], axis=dim)
    return shard


def tap_columns(rimmed, row_count, col_count):
    padded = jnp.pad(rimmed, ((0, 0), (0, 0), (1, 1)))
    stacked = jnp.stack(
        [
            padded[
                :,
                1 + row_shift : 1 + row_shift + row_count,
                1 + col_shift : 1 + col_shift + col_count,
            ]
            for row_shift, col_shift in TAPS
        ],
        axis=0,
    )
    return stacked.reshape(9 * rimmed.shape[0], row_count * col_count)


def per_device(band_strip, conv_weight, gdn_gamma, gdn_beta, cotangent):
    in_local = band_strip.shape[0]
    row_count = band_strip.shape[1]
    col_count = band_strip.shape[2]
    pixels = row_count * col_count
    lat_local = gdn_gamma.shape[0]
    rimmed = extended(band_strip, (("row", 1),), 1)
    columns = tap_columns(rimmed, row_count, col_count)
    shard_piece = lax.all_gather(conv_weight, "row", axis=0, tiled=True)
    flat = shard_piece.reshape(shard_piece.shape[0], 9 * in_local)
    partial_value = jnp.dot(flat, columns, preferred_element_type=jnp.float32)
    pre = lax.psum_scatter(partial_value, "chan", scatter_dimension=0, tiled=True)
    squares_own = (pre * pre).astype(jnp.bfloat16)
    squares = lax.all_gather(squares_own, "chan", axis=0, tiled=True)
    norm_value = gdn_beta[:, None] + jnp.dot(gdn_gamma, squares, preferred_element_type=jnp.float32)
    inverse = lax.rsqrt(norm_value)
    latent = (pre * inverse).astype(jnp.bfloat16)
    upstream = cotangent.reshape(lat_local, pixels).astype(jnp.float32)
    shares = (-0.5 * upstream * pre * inverse * inverse * inverse).astype(jnp.bfloat16)
    gamma_cols = lax.all_to_all(gdn_gamma, "chan", split_axis=1, concat_axis=0, tiled=True)
    shares_all = lax.all_gather(shares, "chan", axis=0, tiled=True)
    back_sum = lax.dot_general(
        gamma_cols, shares_all, (((0,), (0,)), ((), ())), preferred_element_type=jnp.float32
    )
    latent_grad = (upstream * inverse + 2.0 * pre * back_sum).astype(jnp.bfloat16)
    gamma_terms = lax.dot_general(
        shares, squares, (((1,), (1,)), ((), ())), preferred_element_type=jnp.float32
    )
    beta_terms = jnp.sum(shares.astype(jnp.float32), axis=1)
    gamma_total, beta_total = lax.psum((gamma_terms, beta_terms), "row")
    scale_factor = 1.0 / math.sqrt(pixels * lax.axis_size("row"))
    grad_gamma = gamma_total * scale_factor
    grad_beta = beta_total * scale_factor
    grad_all = lax.all_gather(
        latent_grad.reshape(lat_local, row_count, col_count), "chan", axis=0, tiled=True
    )
    grad_rimmed = extended(grad_all, (("row", 1),), 1)
    grad_padded = jnp.pad(grad_rimmed, ((0, 0), (0, 0), (1, 1)))
    initial = jnp.zeros((in_local, pixels), jnp.float32)
    running = initial
    shard_piece = lax.all_gather(conv_weight, "row", axis=0, tiled=True)
    count_rows = shard_piece.shape[0]
    for tap_index, (row_shift, col_shift) in enumerate(TAPS):
        window = grad_padded[
            :, 1 - row_shift : 1 - row_shift + row_count, 1 - col_shift : 1 - col_shift + col_count
        ].reshape(count_rows, pixels)
        running = running + lax.dot_general(
            shard_piece[:, tap_index, :],
            window,
            (((0,), (0,)), ((), ())),
            preferred_element_type=jnp.float32,
        )
    return (
        latent.reshape(lat_local, row_count, col_count),
        running.reshape(in_local, row_count, col_count),
        grad_gamma,
        grad_beta,
    )


def solution(mesh):
    return jax.shard_map(
        per_device,
        mesh=mesh,
        in_specs=(
            P("chan", ("grp", "row"), None),
            P("row", None, "chan"),
            P("chan", None),
            P("chan"),
            P("chan", ("grp", "row"), None),
        ),
        out_specs=(
            P("chan", ("grp", "row"), None),
            P("chan", ("grp", "row"), None),
            P(("grp", "chan"), None),
            P(("grp", "chan")),
        ),
        check_vma=False,
    )
```

profile of v0, /device:TPU:0, one launch (start us, length us, event | category | flops | bytes accessed | tf_op | source)
XLA Modules:
  0.0 275.5 jit_solution(17126695772306795772)
XLA Ops:
  7.2 0.7 all-gather.5.cloned.1.call-update
  8.0 1.2 fusion.48
  9.2 1.3 collective-permute-start.1
  10.5 5.5 %collective-permute-start = (bf16[212,1,128]{2,1,0:T(2,128)(2,1)S(1)}, bf16[212,1,128]{2,1,0:T(2,128)(2,1)S(1)}, u32[]{:S(2)}, u32[]{:S(2)}) collective-permute-start(bf16[212,1,128]{2,1,0:T(2,128)(2,1)S(1)} %get-tuple-element.30), channel_id=1, source_target_pairs={{0,2},{2,4},{4,6},{6,8},{8,10},{10,12},{12,14},{1,3},{3,5},{5,7},{... | collective-permute-start | bytes 162824 | tf_op jit(solution)/shard_map/ppermute | solution.py:17
  16.0 1.1 collective-permute-done.1
  17.1 2.5 collective-permute-done
  19.5 2.1 fusion.22
  21.7 0.3 fusion.43
  22.5 0.4 fusion.39
  23.0 0.3 fusion.37
  23.3 0.4 fusion.35
  23.6 0.8 pad.38
  24.5 0.3 copy.17
  24.8 60.2 %all-gather.5.cloned.1.call-done = bf16[1024,9,212]{0,2,1:T(8,128)(2,1)} async-done(((bf16[128,9,212]{0,2,1:T(8,128)(2,1)}), bf16[1024,9,212]{0,2,1:T(8,128)(2,1)}) %all-gather.5.cloned.1.call-update) | async-done | bytes 3907600 | tf_op jit(solution)/shard_map/all_gather | solution.py:47
  85.0 5.5 %reshape.58 = bf16[1024,1908]{0,1:T(8,128)(2,1)} reshape(bf16[1024,9,212]{0,2,1:T(8,128)(2,1)} %all-gather.5.cloned.1.call-done) | data formatting | bytes 7815168 | tf_op jit(solution)/shard_map/reshape | solution.py:48
  90.5 5.8 %convolution_bitcast_fusion = f32[1024,512]{0,1:T(8,128)} fusion(bf16[1908,512]{1,0:T(8,128)(2,1)S(1)} %bitcast.144, bf16[1024,1908]{0,1:T(8,128)(2,1)} %reshape.58), kind=kOutput, calls=%fused_computation.11 | convolution fusion | flops 2000683008 | bytes 7958528 | tf_op jit(solution)/shard_map/dot_general | solution.py:49
  96.4 7.9 %reduce-scatter.2.cloned.1.call-done = f32[512,512]{0,1:T(8,128)} async-done(((f32[1024,512]{0,1:T(8,128)}), f32[512,512]{0,1:T(8,128)}) %reduce-scatter.2.cloned.1.call-update) | async-done | bytes 1048592 | tf_op jit(solution)/shard_map/reduce_scatter | solution.py:50
  104.3 2.2 multiply_convert_fusion.1
  106.6 1.4 copy.13
  108.0 9.0 %all-gather.7.cloned.1.call-done = bf16[1024,512]{0,1:T(8,128)(2,1)} async-done(((bf16[512,512]{0,1:T(8,128)(2,1)}), bf16[1024,512]{0,1:T(8,128)(2,1)}) %all-gather.7.cloned.1.call-update) | async-done | bytes 1048592 | tf_op jit(solution)/shard_map/all_gather | solution.py:52
  117.0 3.5 %convert_reduce_fusion = (f32[512]{0:T(512)S(1)}, bf16[512,512]{0,1:T(8,128)(2,1)}, f32[512,512]{0,1:T(8,128)}, bf16[512,512]{0,1:T(8,128)(2,1)}) fusion(f32[512,512]{0,1:T(8,128)S(1)} %copy-done.2, f32[512,4,128]{0,2,1:T(8,128)S(1)} %copy.13, bf16[1024,512]{0,1:T(8,128)(2,1)} %all-gather.7.cloned.1.call-done, bf16[512,1024]{1,0:T(8,128)(2,1)S(1)} %copy-done.6, ...), kind=kOutput, calls=%fused_computation.31 | convolution fusion | flops 540016128 | bytes 6295552 | tf_op jit(solution)/shard_map/dot_general | solution.py:53
  120.6 0.5 copy.14
  121.2 4.6 %all_to_all.19 = bf16[512,2,512]{0,2,1:T(8,128)(2,1)S(1)} all-to-all(bf16[512,2,512]{0,2,1:T(8,128)(2,1)S(1)} %bitcast.139), channel_id=1, replica_groups=mesh['grp'=2,'row'=8,'chan'=2] {'chan'}, dimensions={1} | all-to-all | bytes 2097152 | tf_op jit(solution)/shard_map/all_to_all | solution.py:58
  125.7 1.3 copy.15
  127.1 3.9 %all-gather.9.cloned.1.call-done = bf16[1024,512]{0,1:T(8,128)(2,1)} async-done(((bf16[512,512]{0,1:T(8,128)(2,1)}), bf16[1024,512]{0,1:T(8,128)(2,1)}) %all-gather.9.cloned.1.call-update) | async-done | bytes 1048592 | tf_op jit(solution)/shard_map/all_gather | solution.py:59
  130.9 3.5 %fusion.11 = bf16[512,512]{0,1:T(8,128)(2,1)} fusion(f32[512,512]{0,1:T(8,128)} %get-tuple-element.18, bf16[1024,512]{0,1:T(8,128)(2,1)} %all-gather.9.cloned.1.call-done, bf16[1024,512]{1,0:T(8,128)(2,1)} %bitcast.140, f32[512,512]{0,1:T(8,128)S(1)} %copy-done.2), kind=kOutput, calls=%fused_computation.19 | convolution fusion | flops 537919488 | bytes 4718592 | tf_op jit(solution)/shard_map/dot_general | solution.py:60
  134.6 2.0 fusion.49
  136.6 1.0 copy-done.7
  137.6 1.1 copy.16
  138.7 21.8 %psum.15 = f32[512]{0:T(512)S(1)} all-reduce(f32[512]{0:T(512)S(1)} %get-tuple-element.16), channel_id=1, replica_groups=mesh['grp'=2,'row'=8,'chan'=2] {'row'}, use_global_device_ids=true, to_apply=%region_3.4 | all-reduce | flops 512 | bytes 4096 | tf_op jit(solution)/shard_map/psum | solution.py:68
  160.5 0.6 broadcast_multiply_fusion.1
  161.1 1.2 fusion.47
  162.3 1.3 collective-permute-start.3
  163.6 4.7 %collective-permute-start.2 = (bf16[1024,1,128]{0,2,1:T(8,128)(2,1)S(1)}, bf16[1024,1,128]{0,2,1:T(8,128)(2,1)S(1)}, u32[]{:S(2)}, u32[]{:S(2)}) collective-permute-start(bf16[1024,1,128]{0,2,1:T(8,128)(2,1)S(1)} %get-tuple-element.28), channel_id=1, source_target_pairs={{0,2},{2,4},{4,6},{6,8},{8,10},{10,12},{12,14},{1,3},{3,5},{5,7},{... | collective-permute-start | bytes 786440 | tf_op jit(solution)/shard_map/ppermute | solution.py:17
  168.3 89.7 %all-reduce.4.cloned.1.call-done = f32[512,1024]{1,0:T(8,128)} async-done(((f32[512,1024]{1,0:T(8,128)}), f32[512,1024]{1,0:T(8,128)}) %all-reduce.4.cloned.1.call-update) | async-done | bytes 2097168 | tf_op jit(solution)/shard_map/psum | solution.py:68
  258.0 3.4 %broadcast_multiply_fusion = f32[512,1024]{1,0:T(8,128)} fusion(f32[512,1024]{1,0:T(8,128)} %all-reduce.4.cloned.1.call-done), kind=kLoop, calls=%fused_computation.32 | loop fusion | flops 524288 | bytes 4194304 | tf_op jit(solution)/shard_map/mul | solution.py:70
  261.4 0.5 fusion.26
  261.9 0.5 fusion.6
  262.4 1.1 fusion.46
  263.7 0.5 fusion.23
  264.2 0.5 fusion.24
  264.7 0.5 fusion.25
  265.2 0.5 fusion.27
  265.7 0.5 fusion.28
  266.2 0.5 fusion.29
  266.7 0.5 fusion.34
  267.2 0.5 fusion.15
  267.8 0.9 reshape.70
  (37 shorter events, 1.3 us)
Async XLA Ops:
  7.2 14.6 %copy-start.3 = (bf16[212,4,128]{2,1,0:T(4,128)(2,1)S(1)}, bf16[212,4,128]{2,1,0:T(4,128)(2,1)}, u32[]{:S(2)}) copy-start(bf16[212,4,128]{2,1,0:T(4,128)(2,1)} %param.5) | copy-start | bytes 651268
  7.2 77.8 %all-gather.5.cloned.1.call-start = ((), (), s32[]{:S(2)}) async-start(), calls=%async_computation.2 | async-start | bytes 4478976 | tf_op jit(solution)/shard_map/all_gather | solution.py:47
  7.9 96.4 %reduce-scatter.2.cloned.1.call-start = ((), (), s32[]{:S(2)}) async-start(), calls=%async_computation.3 | async-start | bytes 3145728 | tf_op jit(solution)/shard_map/reduce_scatter | solution.py:50
  9.2 7.9 %collective-permute-start.1 = (bf16[212,1,128]{2,1,0:T(2,128)(2,1)S(1)}, bf16[212,1,128]{2,1,0:T(2,128)(2,1)S(1)}, u32[]{:S(2)}, u32[]{:S(2)}) collective-permute-start(bf16[212,1,128]{2,1,0:T(2,128)(2,1)S(1)} %get-tuple-element.31), channel_id=1, source_target_pairs={{2,0},{4,2},{6,4},{8,6},{10,8},{12,10},{14,12},{3,1},{5,3},{7,5},{... | collective-permute-start | bytes 162824 | tf_op jit(solution)/shard_map/ppermute | solution.py:18
  10.5 9.1 %collective-permute-start = (bf16[212,1,128]{2,1,0:T(2,128)(2,1)S(1)}, bf16[212,1,128]{2,1,0:T(2,128)(2,1)S(1)}, u32[]{:S(2)}, u32[]{:S(2)}) collective-permute-start(bf16[212,1,128]{2,1,0:T(2,128)(2,1)S(1)} %get-tuple-element.30), channel_id=1, source_target_pairs={{0,2},{2,4},{4,6},{6,8},{8,10},{10,12},{12,14},{1,3},{3,5},{5,7},{... | collective-permute-start | bytes 162824 | tf_op jit(solution)/shard_map/ppermute | solution.py:17
  96.3 20.7 %copy-start.6 = (bf16[512,1024]{1,0:T(8,128)(2,1)S(1)}, bf16[512,1024]{1,0:T(8,128)(2,1)}, u32[]{:S(2)}) copy-start(bf16[512,1024]{1,0:T(8,128)(2,1)} %param.7) | copy-start | bytes 3145732
  96.4 20.7 %copy-start.8 = (f32[512]{0:T(512)S(1)}, f32[512]{0:T(512)}, u32[]{:S(2)}) copy-start(f32[512]{0:T(512)} %param.8) | copy-start | bytes 6148
  96.4 20.6 %all-gather.7.cloned.1.call-start = ((), (), s32[]{:S(2)}) async-start(), calls=%async_computation.4 | async-start | bytes 1572864 | tf_op jit(solution)/shard_map/all_gather | solution.py:52
  104.3 12.7 %copy-start.2 = (f32[512,512]{0,1:T(8,128)S(1)}, f32[512,512]{0,1:T(8,128)}, u32[]{:S(2)}) copy-start(f32[512,512]{0,1:T(8,128)} %reduce-scatter.2.cloned.1.call-done) | copy-start | bytes 3145732
  106.6 24.4 %all-gather.9.cloned.1.call-start = ((), (), s32[]{:S(2)}) async-start(), calls=%async_computation.5 | async-start | bytes 1572864 | tf_op jit(solution)/shard_map/all_gather | solution.py:59
  120.6 40.5 %all-gather.11.cloned.1.call-start = ((), (), s32[]{:S(2)}) async-start(), calls=%async_computation.6 | async-start | bytes 1572864 | tf_op jit(solution)/shard_map/all_gather | solution.py:72
  130.9 3.6 %copy-start.4 = (bf16[512,512]{0,1:T(8,128)(2,1)S(1)}, bf16[512,512]{0,1:T(8,128)(2,1)}, u32[]{:S(2)}) copy-start(bf16[512,512]{0,1:T(8,128)(2,1)} %get-tuple-element.17) | copy-start | bytes 1572868
  130.9 3.6 %copy-start.5 = (bf16[1024,512]{0,1:T(8,128)(2,1)S(1)}, bf16[1024,512]{0,1:T(8,128)(2,1)}, u32[]{:S(2)}) copy-start(bf16[1024,512]{0,1:T(8,128)(2,1)} %all-gather.7.cloned.1.call-done) | copy-start | bytes 3145732
  134.5 123.5 %all-reduce.4.cloned.1.call-start = ((), (), s32[]{:S(2)}) async-start(), calls=%async_computation.7 | async-start | bytes 4194304 | tf_op jit(solution)/shard_map/psum | solution.py:68
  136.6 1.0 copy-start.7
  161.1 100.2 %copy-start.1 = (bf16[1024,4,128]{0,2,1:T(8,128)(2,1)S(1)}, bf16[1024,4,128]{0,2,1:T(8,128)(2,1)}, u32[]{:S(2)}) copy-start(bf16[1024,4,128]{0,2,1:T(8,128)(2,1)} %all-gather.11.cloned.1.call-done) | copy-start | bytes 3145732
  162.3 99.6 %collective-permute-start.3 = (bf16[1024,1,128]{0,2,1:T(8,128)(2,1)S(1)}, bf16[1024,1,128]{0,2,1:T(8,128)(2,1)S(1)}, u32[]{:S(2)}, u32[]{:S(2)}) collective-permute-start(bf16[1024,1,128]{0,2,1:T(8,128)(2,1)S(1)} %get-tuple-element.29), channel_id=1, source_target_pairs={{2,0},{4,2},{6,4},{8,6},{10,8},{12,10},{14,12},{3,1},{5,3},{7,5},{... | collective-permute-start | bytes 786440 | tf_op jit(solution)/shard_map/ppermute | solution.py:18
  163.6 98.3 %collective-permute-start.2 = (bf16[1024,1,128]{0,2,1:T(8,128)(2,1)S(1)}, bf16[1024,1,128]{0,2,1:T(8,128)(2,1)S(1)}, u32[]{:S(2)}, u32[]{:S(2)}) collective-permute-start(bf16[1024,1,128]{0,2,1:T(8,128)(2,1)S(1)} %get-tuple-element.28), channel_id=1, source_target_pairs={{0,2},{2,4},{4,6},{6,8},{8,10},{10,12},{12,14},{1,3},{3,5},{5,7},{... | collective-permute-start | bytes 786440 | tf_op jit(solution)/shard_map/ppermute | solution.py:17
  258.0 3.4 %copy-start = (bf16[1024,9,212]{0,2,1:T(8,128)(2,1)S(1)}, bf16[1024,9,212]{0,2,1:T(8,128)(2,1)}, u32[]{:S(2)}) copy-start(bf16[1024,9,212]{0,2,1:T(8,128)(2,1)} %all-gather.5.cloned.1.call-done) | copy-start | bytes 11722756
Sparse Core Ops, SparseCore 0:
  10.0 74.9 all-gather.4
  96.5 7.7 reduce-scatter.1
  106.7 10.2 all-gather.6
  120.7 10.1 all-gather.8
  134.6 10.1 all-gather.10
  148.9 109.0 all-reduce.3
where the time goes:
time: 276 us
  waiting for transfers between devices  175 us (63%)
  blocking collectives  26.4 us (10%)
  matrix products  19.4 us (7%)
  local copies, waits for them, and re-layouts  17.9 us (6%)
  between operations  14.4 us (5%)
  starting transfers between devices  13.1 us (5%)
  other arithmetic  9.48 us (3%)
    psum x1, waiting for transfers between devices, per_device(): gamma_total, beta_total = lax.psum((gamma_terms, beta_terms), 'row')  89.7 us
    all_gather x1, waiting for transfers between devices, per_device(): shard_piece = lax.all_gather(conv_weight, 'row', axis=0, tiled=True)  60.2 us
    psum x1, blocking collectives, per_device(): gamma_total, beta_total = lax.psum((gamma_terms, beta_terms), 'row')  21.8 us
    ppermute x2, starting transfers between devices, extended(): before = lax.ppermute(last, axis, up)  10.2 us
    all_gather x1, waiting for transfers between devices, per_device(): squares = lax.all_gather(squares_own, 'chan', axis=0, tiled=True)  8.99 us
    reduce_scatter x1, waiting for transfers between devices, per_device(): lax.psum_scatter(partial_value, 'chan', scatter_dimension=0, tiled=True)  7.88 us
    dot_general x1, matrix products, per_device(): partial_value = jnp.dot(flat, columns, preferred_element_type=jnp.float32)  5.78 us
    reshape x1, local copies, waits for them, and re-layouts, per_device(): flat = shard_piece.reshape(shard_piece.shape[0], 9 * in_local)  5.54 us
  transfers between devices with their start and end apart: 10, of which 7 were waited for; matrix products, arithmetic and copies ran while one was open for 7% of the time, Pallas kernels for 0%

commit v1 on v0

--- a/solution.py
+++ b/solution.py
@@ -44,7 +44,16 @@
     lat_local = gdn_gamma.shape[0]
     rimmed = extended(band_strip, (("row", 1),), 1)
     columns = tap_columns(rimmed, row_count, col_count)
-    shard_piece = lax.all_gather(conv_weight, "row", axis=0, tiled=True)
+    raw_out, vec_out = (lax.axis_size("row"), lax.axis_index("row"))
+    shard_piece, even = (conv_weight, 1)
+    while even < raw_out:
+        high = lax.ppermute(
+            shard_piece, axis_name="row", perm=tuple(((at, at ^ even) for at in range(raw_out)))
+        )
+        left_arr = jnp.concatenate([shard_piece, high], axis=0)
+        x_now = jnp.concatenate([high, shard_piece], axis=0)
+        shard_piece = jnp.where(vec_out & even == 0, left_arr, x_now)
+        even = 2 * even
     flat = shard_piece.reshape(shard_piece.shape[0], 9 * in_local)
     partial_value = jnp.dot(flat, columns, preferred_element_type=jnp.float32)
     pre = lax.psum_scatter(partial_value, "chan", scatter_dimension=0, tiled=True)

time: 276 us -> 408 us (1.48)
  waiting for transfers between devices: 175 us -> 269 us
  other arithmetic: 9.48 us -> 24.6 us
  local copies, waits for them, and re-layouts: 17.9 us -> 27.5 us
  starting transfers between devices: 13.1 us -> 19.7 us
  matrix products: 19.4 us -> 24.1 us
    ppermute x0 -> x3, waiting for transfers between devices: none -> 96.6 us  [per_device(): lax.ppermute(shard_piece, axis_name='row', perm=tuple(((at, at ^ even) fo...]
    select_n x0 -> x4, other arithmetic: none -> 8.17 us  [per_device(): shard_piece = jnp.where(vec_out & even == 0, left_arr, x_now)]
    ppermute x0 -> x3, starting transfers between devices: none -> 7.48 us  [per_device(): lax.ppermute(shard_piece, axis_name='row', perm=tuple(((at, at ^ even) fo...]
    concatenate x3, other arithmetic: 2.73 us -> 9.73 us  [extended(): shard = jnp.concatenate([before, shard, after], axis=dim)]
    concatenate x0 -> x4, local copies, waits for them, and re-layouts: none -> 6.07 us  [per_device(): left_arr = jnp.concatenate([shard_piece, high], axis=0)]
  transfers between devices with their start and end apart: 10 -> 13, of which waited for: 7 -> 9; matrix products, arithmetic and copies ran while one was open for 7% -> 10% of each run, Pallas kernels for 0% -> 0%
where the time goes in v1:
time: 408 us; the launch traced here: 407 us
  waiting for transfers between devices  269 us (66%)
  blocking collectives  28.4 us (7%)
  local copies, waits for them, and re-layouts  27.5 us (7%)
  other arithmetic  24.6 us (6%)
  matrix products  24.1 us (6%)
  starting transfers between devices  19.7 us (5%)
  between operations  14.4 us (4%)
    ppermute x3, waiting for transfers between devices, per_device(): lax.ppermute(shard_piece, axis_name='row', perm=tuple(((at, at ^ even) fo...  96.6 us
    psum x1, waiting for transfers between devices, per_device(): gamma_total, beta_total = lax.psum((gamma_terms, beta_terms), 'row')  92.2 us
    all_gather x1, waiting for transfers between devices, per_device(): shard_piece = lax.all_gather(conv_weight, 'row', axis=0, tiled=True)  56.8 us
    psum x1, blocking collectives, per_device(): gamma_total, beta_total = lax.psum((gamma_terms, beta_terms), 'row')  21.8 us
    reduce_scatter x1, waiting for transfers between devices, per_device(): lax.psum_scatter(partial_value, 'chan', scatter_dimension=0, tiled=True)  10.8 us
    all_gather x1, waiting for transfers between devices, per_device(): squares = lax.all_gather(squares_own, 'chan', axis=0, tiled=True)  10.2 us
    concatenate x3, other arithmetic, extended(): shard = jnp.concatenate([before, shard, after], axis=dim)  9.73 us
    ppermute x2, starting transfers between devices, extended(): before = lax.ppermute(last, axis, up)  9.26 us
  transfers between devices with their start and end apart: 13, of which 9 were waited for; matrix products, arithmetic and copies ran while one was open for 10% of the time, Pallas kernels for 0%

profile of v1, /device:TPU:0, one launch (start us, length us, event | category | flops | bytes accessed | tf_op | source)
XLA Modules:
  0.0 407.5 jit_solution(10096581388426115018)
XLA Ops:
  7.2 3.0 collective-permute-start
  10.3 11.6 %collective-permute-done = bf16[128,9,212]{0,2,1:T(8,128)(2,1)S(1)} collective-permute-done((bf16[128,9,212]{0,2,1:T(8,128)(2,1)}, bf16[128,9,212]{0,2,1:T(8,128)(2,1)S(1)}, u32[]{:S(2)}, u32[]{:S(2)}) %collective-permute-start) | collective-permute-done | bytes 488480 | tf_op jit(solution)/shard_map/ppermute | solution.py:50
  21.8 1.5 maximum_select_fusion.4
  23.3 1.9 collective-permute-start.1
  25.2 0.8 fusion.59
  26.0 1.3 collective-permute-start.4
  27.3 4.6 %collective-permute-start.3 = (bf16[212,1,128]{2,1,0:T(2,128)(2,1)S(1)}, bf16[212,1,128]{2,1,0:T(2,128)(2,1)S(1)}, u32[]{:S(2)}, u32[]{:S(2)}) collective-permute-start(bf16[212,1,128]{2,1,0:T(2,128)(2,1)S(1)} %get-tuple-element.18), channel_id=1, source_target_pairs={{0,2},{2,4},{4,6},{6,8},{8,10},{10,12},{12,14},{1,3},{3,5},{5,7},{... | collective-permute-start | bytes 162824 | tf_op jit(solution)/shard_map/ppermute | solution.py:17
  31.9 0.9 concatenate.58
  32.8 1.3 collective-permute-done.3
  34.2 1.1 fusion.44
  35.6 12.1 %collective-permute-done.1 = bf16[256,9,212]{0,2,1:T(8,128)(2,1)S(1)} collective-permute-done((bf16[256,9,212]{0,2,1:T(8,128)(2,1)S(1)}, bf16[256,9,212]{0,2,1:T(8,128)(2,1)S(1)}, u32[]{:S(2)}, u32[]{:S(2)}) %collective-permute-start.1) | collective-permute-done | bytes 976928 | tf_op jit(solution)/shard_map/ppermute | solution.py:50
  47.7 1.9 maximum_select_fusion.2
  49.6 2.6 collective-permute-start.2
  53.8 0.8 pad.58
  54.7 1.6 copy.23
  56.3 0.9 concatenate.59
  57.1 1.5 maximum_select_fusion.5
  58.6 1.1 concatenate.64
  59.7 3.4 maximum_select_fusion.3
  63.1 72.9 %collective-permute-done.2 = bf16[512,9,212]{0,2,1:T(8,128)(2,1)} collective-permute-done((bf16[512,9,212]{0,2,1:T(8,128)(2,1)}, bf16[512,9,212]{0,2,1:T(8,128)(2,1)}, u32[]{:S(2)}, u32[]{:S(2)}) %collective-permute-start.2) | collective-permute-done | bytes 1953824 | tf_op jit(solution)/shard_map/ppermute | solution.py:50
  136.0 3.2 concatenate.69
  139.2 7.0 %fusion.6 = f32[1024,512]{1,0:T(8,128)} fusion(bf16[1908,512]{1,0:T(8,128)(2,1)S(1)} %bitcast.146, bf16[512,1908]{0,1:T(8,128)(2,1)} %concatenate.69, bf16[512,1908]{0,1:T(8,128)(2,1)} %maximum_select_fusion.3, pred[]{:T(512)S(6)} %eq.9), kind=kOutput, calls=%fused_computation.9 | convolution fusion | flops 2018267136 | bytes 7958529 | tf_op jit(solution)/shard_map/dot_general | solution.py:58
  146.3 10.8 %reduce-scatter.2.cloned.1.call-done = f32[512,512]{1,0:T(8,128)} async-done(((f32[1024,512]{1,0:T(8,128)}), f32[512,512]{1,0:T(8,128)}) %reduce-scatter.2.cloned.1.call-update) | async-done | bytes 1048592 | tf_op jit(solution)/shard_map/reduce_scatter | solution.py:59
  157.1 2.2 multiply_convert_fusion.1
  159.6 10.2 %all-gather.5.cloned.1.call-done = bf16[1024,512]{1,0:T(8,128)(2,1)} async-done(((bf16[512,512]{1,0:T(8,128)(2,1)}), bf16[1024,512]{1,0:T(8,128)(2,1)}) %all-gather.5.cloned.1.call-update) | async-done | bytes 1048592 | tf_op jit(solution)/shard_map/all_gather | solution.py:61
  169.8 3.2 convert_reduce_fusion
  173.1 2.3 copy.18
  175.4 6.6 %all_to_all.19 = bf16[512,2,512]{0,2,1:T(8,128)(2,1)} all-to-all(bf16[512,2,512]{0,2,1:T(8,128)(2,1)} %bitcast.144), channel_id=1, replica_groups=mesh['grp'=2,'row'=8,'chan'=2] {'chan'}, dimensions={1} | all-to-all | bytes 2097152 | tf_op jit(solution)/shard_map/all_to_all | solution.py:67
  182.0 2.3 copy.19
  184.2 3.4 fusion.38
  187.6 2.1 reshape.69
  190.0 3.1 fusion.60
  193.7 21.8 %psum.15 = f32[512]{0:T(512)S(1)} all-reduce(f32[512]{0:T(512)S(1)} %get-tuple-element.4), channel_id=1, replica_groups=mesh['grp'=2,'row'=8,'chan'=2] {'row'}, use_global_device_ids=true, to_apply=%region_3.4 | all-reduce | flops 512 | bytes 4096 | tf_op jit(solution)/shard_map/psum | solution.py:77
  215.5 0.6 broadcast_multiply_fusion.1
  216.1 0.9 reshape.68
  217.0 2.6 fusion.58
  219.7 1.3 collective-permute-start.6
  221.0 4.7 %collective-permute-start.5 = (bf16[1024,1,128]{2,1,0:T(2,128)(2,1)S(1)}, bf16[1024,1,128]{2,1,0:T(2,128)(2,1)S(1)}, u32[]{:S(2)}, u32[]{:S(2)}) collective-permute-start(bf16[1024,1,128]{2,1,0:T(2,128)(2,1)S(1)} %get-tuple-element.16), channel_id=1, source_target_pairs={{0,2},{2,4},{4,6},{6,8},{8,10},{10,12},{12,14},{1,3},{3,5},{5,7},{... | collective-permute-start | bytes 786440 | tf_op jit(solution)/shard_map/ppermute | solution.py:17
  225.7 92.2 %all-reduce.4.cloned.1.call-done = f32[512,1024]{1,0:T(8,128)} async-done(((f32[512,1024]{1,0:T(8,128)}), f32[512,1024]{1,0:T(8,128)}) %all-reduce.4.cloned.1.call-update) | async-done | bytes 2097168 | tf_op jit(solution)/shard_map/psum | solution.py:77
  317.9 3.2 broadcast_multiply_fusion
  321.1 3.3 pad_maximum_fusion
  324.5 5.3 %fusion.5 = bf16[1024,6,130]{2,1,0:T(8,128)(2,1)S(1)} fusion(bf16[1024,1,128]{2,1,0:T(2,128)(2,1)S(1)} %collective-permute-done.6, bf16[1024,4,128]{2,1,0:T(4,128)(2,1)S(1)} %copy-done.1, bf16[1024,1,128]{2,1,0:T(2,128)(2,1)S(1)} %collective-permute-done.5), kind=kLoop, calls=%fused_computation.7 | loop fusion | flops 9584640 | bytes 3170304 | tf_op jit(solution)/shard_map/concatenate | solution.py:19
  329.8 4.8 %fusion.57 = (bf16[1024,4,128]{2,1,0:T(4,128)(2,1)S(1)}, bf16[1024,4,128]{2,1,0:T(4,128)(2,1)S(1)}, bf16[1024,4,128]{2,1,0:T(4,128)(2,1)}, bf16[1024,4,128]{2,1,...) fusion(bf16[1024,6,130]{2,1,0:T(8,128)(2,1)S(1)} %fusion.5), kind=kLoop, calls=%fused_computation.103 | loop fusion | bytes 12582912 | tf_op jit(solution)/shard_map/slice | solution.py:91
  334.6 56.8 %all-gather.11.cloned.1.call-done = bf16[1024,9,212]{0,2,1:T(8,128)(2,1)} async-done(((bf16[128,9,212]{0,2,1:T(8,128)(2,1)}), bf16[1024,9,212]{0,2,1:T(8,128)(2,1)}) %all-gather.11.cloned.1.call-update) | async-done | bytes 3907600 | tf_op jit(solution)/shard_map/all_gather | solution.py:88
  391.4 1.9 fusion.34
  393.3 1.7 convolution_add_fusion.8
  395.0 1.4 convolution_add_fusion.7
  399.7 0.9 reshape.79
  (65 shorter events, 6.5 us)
Async XLA Ops:
  7.2 24.7 %copy-start.3 = (bf16[128,9,212]{0,2,1:T(8,128)(2,1)S(1)}, bf16[128,9,212]{0,2,1:T(8,128)(2,1)}, u32[]{:S(2)}) copy-start(bf16[128,9,212]{0,2,1:T(8,128)(2,1)} %param.6) | copy-start | bytes 1465348
  7.2 18.0 %copy-start.2 = (bf16[212,4,128]{2,1,0:T(4,128)(2,1)S(1)}, bf16[212,4,128]{2,1,0:T(4,128)(2,1)}, u32[]{:S(2)}) copy-start(bf16[212,4,128]{2,1,0:T(4,128)(2,1)} %param.5) | copy-start | bytes 651268
  7.2 150.0 %reduce-scatter.2.cloned.1.call-start = ((), (), s32[]{:S(2)}) async-start(), calls=%async_computation.2 | async-start | bytes 3145728 | tf_op jit(solution)/shard_map/reduce_scatter | solution.py:59
  7.2 14.6 %collective-permute-start = (bf16[128,9,212]{0,2,1:T(8,128)(2,1)}, bf16[128,9,212]{0,2,1:T(8,128)(2,1)S(1)}, u32[]{:S(2)}, u32[]{:S(2)}) collective-permute-start(bf16[128,9,212]{0,2,1:T(8,128)(2,1)} %param.6), channel_id=1, source_target_pairs={{0,2},{2,0},{4,6},{6,4},{8,10},{10,8},{12,14},{14,12},{1,3},{3,1},... | collective-permute-start | bytes 1465352 | tf_op jit(solution)/shard_map/ppermute | solution.py:50
  23.3 24.4 %collective-permute-start.1 = (bf16[256,9,212]{0,2,1:T(8,128)(2,1)S(1)}, bf16[256,9,212]{0,2,1:T(8,128)(2,1)S(1)}, u32[]{:S(2)}, u32[]{:S(2)}) collective-permute-start(bf16[256,9,212]{0,2,1:T(8,128)(2,1)S(1)} %maximum_select_fusion.4), channel_id=1, source_target_pairs={{0,4},{2,6},{4,0},{6,2},{8,12},{10,14},{12,8},{14,10},{1,5},{3,7},... | collective-permute-start | bytes 2930696 | tf_op jit(solution)/shard_map/ppermute | solution.py:50
  26.0 6.8 %collective-permute-start.4 = (bf16[212,1,128]{2,1,0:T(2,128)(2,1)}, bf16[212,1,128]{2,1,0:T(2,128)(2,1)S(1)}, u32[]{:S(2)}, u32[]{:S(2)}) collective-permute-start(bf16[212,1,128]{2,1,0:T(2,128)(2,1)} %get-tuple-element.19), channel_id=1, source_target_pairs={{2,0},{4,2},{6,4},{8,6},{10,8},{12,10},{14,12},{3,1},{5,3},{7,5},{... | collective-permute-start | bytes 162824 | tf_op jit(solution)/shard_map/ppermute | solution.py:18
  27.3 6.8 %collective-permute-start.3 = (bf16[212,1,128]{2,1,0:T(2,128)(2,1)S(1)}, bf16[212,1,128]{2,1,0:T(2,128)(2,1)S(1)}, u32[]{:S(2)}, u32[]{:S(2)}) collective-permute-start(bf16[212,1,128]{2,1,0:T(2,128)(2,1)S(1)} %get-tuple-element.18), channel_id=1, source_target_pairs={{0,2},{2,4},{4,6},{6,8},{8,10},{10,12},{12,14},{1,3},{3,5},{5,7},{... | collective-permute-start | bytes 162824 | tf_op jit(solution)/shard_map/ppermute | solution.py:17
  49.6 86.4 %collective-permute-start.2 = (bf16[512,9,212]{0,2,1:T(8,128)(2,1)}, bf16[512,9,212]{0,2,1:T(8,128)(2,1)}, u32[]{:S(2)}, u32[]{:S(2)}) collective-permute-start(bf16[512,9,212]{0,2,1:T(8,128)(2,1)} %maximum_select_fusion.2), channel_id=1, source_target_pairs={{0,8},{2,10},{4,12},{6,14},{8,0},{10,2},{12,4},{14,6},{1,9},{3,11}... | collective-permute-start | bytes 5861384 | tf_op jit(solution)/shard_map/ppermute | solution.py:50
  54.7 2.5 copy-start.7
  63.1 76.1 %copy-start.6 = (bf16[239,8,4,128]{3,1,2,0:T(8,128)(2,1)S(1)}, bf16[239,8,4,128]{3,1,2,0:T(8,128)(2,1)}, u32[]{:S(2)}) copy-start(bf16[239,8,4,128]{3,1,2,0:T(8,128)(2,1)} %copy.23) | copy-start | bytes 5873668
  146.2 13.2 %copy-start.13 = (bf16[512,4,128]{2,1,0:T(4,128)(2,1)S(1)}, bf16[512,4,128]{2,1,0:T(4,128)(2,1)}, u32[]{:S(2)}) copy-start(bf16[512,4,128]{2,1,0:T(4,128)(2,1)} %param.9) | copy-start | bytes 1572868
  146.3 23.6 %copy-start.14 = (f32[512]{0:T(512)S(1)}, f32[512]{0:T(512)}, u32[]{:S(2)}) copy-start(f32[512]{0:T(512)} %param.8) | copy-start | bytes 6148
  146.3 23.5 %all-gather.5.cloned.1.call-start = ((), (), s32[]{:S(2)}) async-start(), calls=%async_computation.3 | async-start | bytes 1572864 | tf_op jit(solution)/shard_map/all_gather | solution.py:61
  157.1 12.7 %copy-start = (f32[512,512]{1,0:T(8,128)S(1)}, f32[512,512]{1,0:T(8,128)}, u32[]{:S(2)}) copy-start(f32[512,512]{1,0:T(8,128)} %reduce-scatter.2.cloned.1.call-done) | copy-start | bytes 3145732
  159.4 24.9 %all-gather.7.cloned.1.call-start = ((), (), s32[]{:S(2)}) async-start(), calls=%async_computation.4 | async-start | bytes 1572864 | tf_op jit(solution)/shard_map/all_gather | solution.py:68
  173.0 44.0 %all-gather.9.cloned.1.call-start = ((), (), s32[]{:S(2)}) async-start(), calls=%async_computation.5 | async-start | bytes 1572864 | tf_op jit(solution)/shard_map/all_gather | solution.py:81
  187.6 2.4 copy-start.4
  189.8 128.2 %all-reduce.4.cloned.1.call-start = ((), (), s32[]{:S(2)}) async-start(), calls=%async_computation.7 | async-start | bytes 4194304 | tf_op jit(solution)/shard_map/psum | solution.py:77
  193.1 23.0 %copy-start.5 = (bf16[512,512]{1,0:T(8,128)(2,1)S(1)}, bf16[512,512]{1,0:T(8,128)(2,1)}, u32[]{:S(2)}) copy-start(bf16[512,512]{1,0:T(8,128)(2,1)} %get-tuple-element.13) | copy-start | bytes 1572868
  193.1 198.2 %all-gather.11.cloned.1.call-start = ((), (), s32[]{:S(2)}) async-start(), calls=%async_computation.6 | async-start | bytes 4478976 | tf_op jit(solution)/shard_map/all_gather | solution.py:88
  219.7 101.5 %collective-permute-start.6 = (bf16[1024,1,128]{2,1,0:T(2,128)(2,1)S(1)}, bf16[1024,1,128]{2,1,0:T(2,128)(2,1)S(1)}, u32[]{:S(2)}, u32[]{:S(2)}) collective-permute-start(bf16[1024,1,128]{2,1,0:T(2,128)(2,1)S(1)} %get-tuple-element.17), channel_id=1, source_target_pairs={{2,0},{4,2},{6,4},{8,6},{10,8},{12,10},{14,12},{3,1},{5,3},{7,5},{... | collective-permute-start | bytes 786440 | tf_op jit(solution)/shard_map/ppermute | solution.py:18
  221.0 100.2 %copy-start.1 = (bf16[1024,4,128]{2,1,0:T(4,128)(2,1)S(1)}, bf16[1024,4,128]{2,1,0:T(4,128)(2,1)}, u32[]{:S(2)}) copy-start(bf16[1024,4,128]{2,1,0:T(4,128)(2,1)} %all-gather.9.cloned.1.call-done) | copy-start | bytes 3145732
  221.0 100.2 %collective-permute-start.5 = (bf16[1024,1,128]{2,1,0:T(2,128)(2,1)S(1)}, bf16[1024,1,128]{2,1,0:T(2,128)(2,1)S(1)}, u32[]{:S(2)}, u32[]{:S(2)}) collective-permute-start(bf16[1024,1,128]{2,1,0:T(2,128)(2,1)S(1)} %get-tuple-element.16), channel_id=1, source_target_pairs={{0,2},{2,4},{4,6},{6,8},{8,10},{10,12},{12,14},{1,3},{3,5},{5,7},{... | collective-permute-start | bytes 786440 | tf_op jit(solution)/shard_map/ppermute | solution.py:17
  391.3 1.9 copy-start.12
  391.3 3.7 copy-start.10
  391.4 5.1 %copy-start.15 = (bf16[1024,9,212]{0,2,1:T(8,128)(2,1)S(1)}, bf16[1024,9,212]{0,2,1:T(8,128)(2,1)}, u32[]{:S(2)}) copy-start(bf16[1024,9,212]{0,2,1:T(8,128)(2,1)} %all-gather.11.cloned.1.call-done) | copy-start | bytes 11722756
  393.2 3.2 copy-start.9
  396.5 1.2 copy-start.8
  397.7 1.2 copy-start.11
Sparse Core Ops, SparseCore 0:
  146.4 10.7 reduce-scatter.1
  159.5 10.2 all-gather.4
  173.2 10.1 all-gather.6
  189.9 10.1 all-gather.8
  204.1 113.7 all-reduce.3
  319.8 71.4 all-gather.10
